TPU v7x, 128 devices: a whole 4x4x4 slice. The times are simulated.
128 devices in a mesh: row: 8 (over x, core), col: 16 (over z, y).
Axes of the slice: x: 4, y: 4, z: 4, core: 2. Of those that a mesh axis runs over, the one named last changes fastest.
Arguments:
- unit_factor: float32 [4, 1024, 2, 2048], P(None, 'row', None, 'col'), may hold values from -0.125 to 0.125
- pivot_inverse: float32 [4, 1024, 2, 2048], P(None, 'row', None, 'col')
- supernode: int32 [32], replicated, may hold values from 0 to 2, never falling along the last dimension, each value on 1 to 16 neighbouring positions
- row_bits: int32 [32, 2], replicated, may hold values 0 or 1
Outputs:
- inverse_blocks: float32 [4, 1024, 2, 2048], P(None, 'row', None, 'col')
Inputs may be any that keep to these rules, and one draw needn't show every extreme that they name: The supernode index never decreases from one block to the next; each supernode has 1 to 16 blocks, one of them exactly 16.
All inputs are finite; a program needn't handle non-finite values.
Results may differ from a plain program's by a relative error of at most 0.0001.
Values sent between devices are 32-bit elements; how exact they have to be, the bound alone decides.
No kernel may reach another device: no remote copies, remote signals or barrier semaphores. Data moves between devices by JAX's collectives and lax.ppermute only.
A program may use at most 128 MiB of HBM per device.

v0:
```python
import jax
import jax.numpy as jnp
from jax import lax
from jax.sharding import PartitionSpec as P

SUPERNODES = 3


def pick(table, index):
    hits = index[:, None] == jnp.arange(table.shape[0])[None, :]
    return jnp.sum(jnp.where(hits, table[None, :], 0.0), axis=1)


def shards(unit_factor, pivot_inverse, supernode, row_bits):
    n_row = lax.axis_size("row")
    n_col = lax.axis_size("col")
    brows, width, bcols, _ = unit_factor.shape
    whole = brows * n_row * width
    row_ids = jnp.arange(brows) * n_row + lax.axis_index("row")
    col_ids = jnp.arange(bcols) * n_col + lax.axis_index("col")
    highest = lax.Precision.HIGHEST

    def member_of(level):
        return (supernode == level).astype(jnp.float32)

    def local_mask(for_rows, for_cols):
        return (
            pick(for_rows, row_ids)[:, None, None, None]
            * pick(for_cols, col_ids)[None, None, :, None]
        )

    last = SUPERNODES - 1
    inverse = pivot_inverse * local_mask(member_of(last), member_of(last))
    column_panel = lax.all_gather(unit_factor, "row", axis=1, tiled=True).reshape(
        whole, bcols * width
    )
    row_panel = lax.all_gather(unit_factor, "col", axis=3, tiled=True).reshape(brows * width, whole)
    for level in range(last - 1, -1, -1):
        member = member_of(level)
        inside = jnp.logical_and(supernode > level, jnp.all(row_bits[:, level:] == 1, axis=1))
        struct = inside.astype(jnp.float32)
        ancestors = inverse * local_mask(struct, struct)
        ucols = (
            column_panel
            * jnp.repeat(struct, width)[:, None]
            * jnp.repeat(pick(member, col_ids), width)[None, :]
        )
        urows = (
            row_panel
            * jnp.repeat(pick(struct, row_ids), width)[:, None]
            * jnp.repeat(member, width)[None, :]
        )
        stacked = ucols.reshape(bcols, n_col * width, bcols * width)
        spread = urows.reshape(brows * width, brows, n_row * width)
        flat_ancestors = ancestors.reshape(brows * width, bcols * width)
        image = jnp.einsum(
            "kajp,jpl->kal",
            lax.all_gather(ancestors, "col", axis=3, tiled=True),
            stacked,
            precision=highest,
            preferred_element_type=jnp.float32,
        )
        flat_image = image.reshape(brows * width, bcols * width)
        update = lax.psum_scatter(
            jnp.einsum(
                "hkp,hl->pkl",
                spread,
                flat_image - flat_ancestors,
                precision=highest,
                preferred_element_type=jnp.float32,
            ),
            "row",
            scatter_dimension=0,
            tiled=True,
        )
        update = jnp.transpose(update, (1, 0, 2)).reshape(brows, width, bcols, width)
        inverse = (
            inverse
            - image.reshape(brows, width, bcols, width)
            + update
            + pivot_inverse * local_mask(member, member)
        )
    return inverse


def solution(mesh):
    in_specs = (P(None, "row", None, "col"), P(None, "row", None, "col"), P(), P())
    out_specs = P(None, "row", None, "col")
    return jax.shard_map(shards, mesh=mesh, in_specs=in_specs, out_specs=out_specs, check_vma=False)
```

profile of v0, /device:TPU:0, one launch (start us, length us, event | category | flops | bytes accessed | tf_op | source)
XLA Modules:
  0.0 454.2 jit_solution(7438462885738137960)
XLA Ops:
  6.5 0.7 all-gather.7.cloned.1.call-update
  7.3 0.7 all-gather.9.cloned.1.call-update
  8.1 0.7 compare_reduce_fusion
  8.8 0.7 compare_convert_fusion.2
  9.5 0.2 select_reduce_fusion
  9.7 0.3 select_reduce_fusion.5
  10.1 2.0 multiply_multiply_fusion.2
  12.1 1.2 copy.34
  13.6 0.2 copy.35
  14.1 29.4 %all-gather.7.cloned.1.call-done = f32[4,1024,2,128]{3,2,1,0:T(2,128)} async-done(((f32[4,128,2,128]{3,2,1,0:T(2,128)}), f32[4,1024,2,128]{3,2,1,0:T(2,128)}) %all-gather.7.cloned.1.call-update) | async-done | bytes 4194320 | tf_op jit(solution)/shard_map/all_gather | solution.py:34
  43.6 6.5 %reshape.289 = f32[2,2048,256]{2,1,0:T(8,128)} reshape(f32[4,1024,2,128]{3,2,1,0:T(2,128)} %all-gather.7.cloned.1.call-done) | data formatting | bytes 8388608 | tf_op jit(solution)/shard_map/reshape | solution.py:34
  50.0 113.4 %all-gather.9.cloned.1.call-done = f32[4,128,2,2048]{3,2,1,0:T(2,128)} async-done(((f32[4,128,2,128]{3,2,1,0:T(2,128)}), f32[4,128,2,2048]{3,2,1,0:T(2,128)}) %all-gather.9.cloned.1.call-update) | async-done | bytes 8388624 | tf_op jit(solution)/shard_map/all_gather | solution.py:37
  163.4 10.5 %multiply_multiply_fusion = (f32[4,128,2,2048]{3,2,1,0:T(2,128)}, f32[4,128,2,2048]{3,2,1,0:T(2,128)}) fusion(f32[4,128,2,2048]{3,2,1,0:T(2,128)} %all-gather.9.cloned.1.call-done, f32[4]{0:T(128)S(1)} %get-tuple-element.6, f32[2,2048]{1,0:T(2,128)S(1)} %mul.288, f32[2,2048]{1,0:T(2,128)S(1)} %mul.267, f32[4]{0:T(128)S(1)} %get-tuple-element.8), kind=kLoop, calls=%fused_computation.4 | loop fusion | flops 8388608 | bytes 25198624 | tf_op jit(solution)/shard_map/mul | solution.py:49
  173.9 12.4 %mul.270 = f32[512,4,1024]{2,1,0:T(4,128)} reshape(f32[4,128,2,2048]{3,2,1,0:T(2,128)} %get-tuple-element.16) | data formatting | bytes 16777216 | tf_op jit(solution)/shard_map/mul | solution.py:49
  186.4 57.4 %all-gather.5.cloned.1.call-done = f32[4,128,2,2048]{3,1,2,0:T(8,128)} async-done(((f32[4,128,2,128]{3,1,2,0:T(8,128)}), f32[4,128,2,2048]{3,1,2,0:T(8,128)}) %all-gather.5.cloned.1.call-update) | async-done | bytes 8388624 | tf_op jit(solution)/shard_map/all_gather | solution.py:58
  243.8 11.4 %fusion.29 = (f32[4,128,256]{2,1,0:T(8,128)S(1)}, f32[4,128,256]{2,1,0:T(8,128)S(1)}) fusion(f32[4,128,256]{2,1,0:T(8,128)S(1)} %copy.35, f32[4,128,2,2048]{3,1,2,0:T(8,128)} %all-gather.5.cloned.1.call-done, f32[2,2048,256]{2,1,0:T(8,128)} %reshape.289, f32[256]{0:T(256)S(1)} %broadcast_bitcast_fusion.3, f32[2,2048]{1,0:T(2,128)S(1)} %bitcast.70), kind=kOutput, calls=%fused_computation.58 | convolution fusion | flops 6444679168 | bytes 14173184 | tf_op jit(solution)/shard_map/kajp,jpl->kal/dot_general | solution.py:56
  255.2 12.4 %fusion.12 = f32[1024,4,256]{0,2,1:T(8,128)} fusion(f32[512,256,1]{1,0,2:T(8,128)S(1)} %bitcast.63, f32[512,4,1024]{2,1,0:T(4,128)S(1)} %copy-done.1), kind=kOutput, calls=%fused_computation.14 | convolution fusion | flops 6442450944 | bytes 13107200 | tf_op jit(solution)/shard_map/hkp,hl->pkl/dot_general | solution.py:65
  268.0 0.2 copy.33
  268.2 36.7 %reduce-scatter.3.cloned.1.call-done = f32[128,4,256]{0,2,1:T(8,128)} async-done(((f32[1024,4,256]{0,2,1:T(8,128)}), f32[128,4,256]{0,2,1:T(8,128)}) %reduce-scatter.3.cloned.1.call-update) | async-done | bytes 524304 | tf_op jit(solution)/shard_map/reduce_scatter | solution.py:64
  304.9 1.2 copy.38
  306.2 1.0 broadcast_multiply_fusion
  307.5 12.6 %mul.291 = f32[512,4,1024]{2,1,0:T(4,128)} reshape(f32[4,128,2,2048]{3,2,1,0:T(2,128)} %get-tuple-element.15) | data formatting | bytes 16777216 | tf_op jit(solution)/shard_map/mul | solution.py:49
  320.1 0.2 copy.42
  320.3 0.2 copy.43
  320.5 63.2 %all-gather.11.cloned.1.call-done = f32[4,128,2,2048]{3,1,2,0:T(8,128)} async-done(((f32[4,128,2,128]{3,1,2,0:T(8,128)}), f32[4,128,2,2048]{3,1,2,0:T(8,128)}) %all-gather.11.cloned.1.call-update) | async-done | bytes 8388624 | tf_op jit(solution)/shard_map/all_gather | solution.py:58
  383.7 11.4 %fusion.30 = (f32[4,128,256]{2,1,0:T(8,128)S(1)}, f32[4,128,256]{2,1,0:T(8,128)S(1)}) fusion(f32[4,128,256]{2,1,0:T(8,128)S(1)} %copy.43, f32[4,128,2,2048]{3,1,2,0:T(8,128)} %all-gather.11.cloned.1.call-done, f32[2,2048,256]{2,1,0:T(8,128)} %reshape.289, f32[256]{0:T(256)S(1)} %broadcast_bitcast_fusion.2, f32[2,2048]{1,0:T(2,128)S(1)} %bitcast.71), kind=kOutput, calls=%fused_computation.59 | convolution fusion | flops 6444679168 | bytes 14173184 | tf_op jit(solution)/shard_map/kajp,jpl->kal/dot_general | solution.py:56
  395.1 12.2 %fusion.15 = f32[1024,4,256]{0,2,1:T(8,128)} fusion(f32[512,256,1]{1,0,2:T(8,128)S(1)} %bitcast.62, f32[512,4,1024]{2,1,0:T(4,128)S(1)} %copy-done), kind=kOutput, calls=%fused_computation.15 | convolution fusion | flops 6442450944 | bytes 13107200 | tf_op jit(solution)/shard_map/hkp,hl->pkl/dot_general | solution.py:65
  407.7 0.2 copy.41
  407.9 36.8 %reduce-scatter.5.cloned.1.call-done = f32[128,4,256]{0,2,1:T(8,128)} async-done(((f32[1024,4,256]{0,2,1:T(8,128)}), f32[128,4,256]{0,2,1:T(8,128)}) %reduce-scatter.5.cloned.1.call-update) | async-done | bytes 524304 | tf_op jit(solution)/shard_map/reduce_scatter | solution.py:64
  444.6 1.2 copy.46
  445.9 0.3 multiply_add_fusion
  446.2 1.2 copy.48
  (39 shorter events, 1.7 us)
Async XLA Ops:
  6.5 37.0 %all-gather.7.cloned.1.call-start = ((), (), s32[]{:S(2)}) async-start(), calls=%async_computation.3 | async-start | bytes 4718592 | tf_op jit(solution)/shard_map/all_gather | solution.py:34
  7.3 156.2 %all-gather.9.cloned.1.call-start = ((), (), s32[]{:S(2)}) async-start(), calls=%async_computation.4 | async-start | bytes 8912896 | tf_op jit(solution)/shard_map/all_gather | solution.py:37
  8.0 235.8 %all-gather.5.cloned.1.call-start = ((), (), s32[]{:S(2)}) async-start(), calls=%async_computation.2 | async-start | bytes 8912896 | tf_op jit(solution)/shard_map/all_gather | solution.py:58
  12.0 292.9 %reduce-scatter.3.cloned.1.call-start = ((), (), s32[]{:S(2)}) async-start(), calls=%async_computation.5 | async-start | bytes 4718592 | tf_op jit(solution)/shard_map/reduce_scatter | solution.py:64
  243.8 11.5 %copy-start.1 = (f32[512,4,1024]{2,1,0:T(4,128)S(1)}, f32[512,4,1024]{2,1,0:T(4,128)}, u32[]{:S(2)}) copy-start(f32[512,4,1024]{2,1,0:T(4,128)} %mul.270) | copy-start | bytes 25165828
  255.2 50.9 %copy-start.3 = (f32[4,128,2,128]{3,2,1,0:T(2,128)S(1)}, f32[4,128,2,128]{3,2,1,0:T(2,128)}, u32[]{:S(2)}) copy-start(f32[4,128,2,128]{3,2,1,0:T(2,128)} %param.5) | copy-start | bytes 1572868
  267.7 116.0 %all-gather.11.cloned.1.call-start = ((), (), s32[]{:S(2)}) async-start(), calls=%async_computation.6 | async-start | bytes 8912896 | tf_op jit(solution)/shard_map/all_gather | solution.py:58
  307.2 137.4 %reduce-scatter.5.cloned.1.call-start = ((), (), s32[]{:S(2)}) async-start(), calls=%async_computation.7 | async-start | bytes 4718592 | tf_op jit(solution)/shard_map/reduce_scatter | solution.py:64
  307.5 12.6 %copy-start.2 = (f32[4,128,2,128]{3,1,2,0:T(8,128)S(1)}, f32[4,128,2,128]{3,1,2,0:T(8,128)}, u32[]{:S(2)}) copy-start(f32[4,128,2,128]{3,1,2,0:T(8,128)} %broadcast_multiply_fusion) | copy-start | bytes 1572868
  383.7 11.4 %copy-start = (f32[512,4,1024]{2,1,0:T(4,128)S(1)}, f32[512,4,1024]{2,1,0:T(4,128)}, u32[]{:S(2)}) copy-start(f32[512,4,1024]{2,1,0:T(4,128)} %mul.291) | copy-start | bytes 25165828
Sparse Core Ops, SparseCore 0:
  9.0 34.4 all-gather.6
  45.7 117.7 all-gather.8
  165.6 78.1 all-gather.4
  267.8 37.0 reduce-scatter.2
  307.3 76.3 all-gather.10
  407.5 37.0 reduce-scatter.4
where the time goes:
time: 455 us; the launch traced here: 454 us
  waiting for transfers between devices  338 us (74%)
  matrix products  47.5 us (10%)
  local copies, waits for them, and re-layouts  38.6 us (8%)
  other arithmetic  15.9 us (3%)
  between operations  13.6 us (3%)
    all_gather x2, waiting for transfers between devices, shards(): lax.all_gather(ancestors, 'col', axis=3, tiled=True)  121 us
    all_gather x1, waiting for transfers between devices, shards(): lax.all_gather(unit_factor, 'col', axis=3, tiled=True)  113 us
    reduce_scatter x2, waiting for transfers between devices, shards(): lax.psum_scatter(jnp.einsum('hkp,hl->pkl', spread, flat_image - flat_ance...  73.5 us
    all_gather x1, waiting for transfers between devices, shards(): lax.all_gather(unit_factor, 'row', axis=1, tiled=True)  29.4 us
    mul x4, local copies, waits for them, and re-layouts, shards(): row_panel * jnp.repeat(pick(struct, row_ids), width)[:, None]  25.1 us
    dot_general x2, matrix products, shards(): jnp.einsum('hkp,hl->pkl', spread, flat_image - flat_ancestors, precision=...  24.6 us
    dot_general x2, matrix products, shards(): jnp.einsum('kajp,jpl->kal', lax.all_gather(ancestors, 'col', axis=3, tile...  22.9 us
    mul x1, other arithmetic, shards(): row_panel * jnp.repeat(pick(struct, row_ids), width)[:, None]  10.5 us
  transfers between devices with their start and end apart: 6, of which 6 were waited for; matrix products, arithmetic and copies ran while one was open for 11% of the time, Pallas kernels for 0%

commit v1 on v0

--- a/solution.py
+++ b/solution.py
@@ -2,6 +2,7 @@
 import jax.numpy as jnp
 from jax import lax
 from jax.sharding import PartitionSpec as P
+from jax.lax import axis_index, axis_size, ppermute
 
 SUPERNODES = 3
 
@@ -53,12 +54,40 @@
         stacked = ucols.reshape(bcols, n_col * width, bcols * width)
         spread = urows.reshape(brows * width, brows, n_row * width)
         flat_ancestors = ancestors.reshape(brows * width, bcols * width)
-        image = jnp.einsum(
-            "kajp,jpl->kal",
-            lax.all_gather(ancestors, "col", axis=3, tiled=True),
-            stacked,
-            precision=highest,
-            preferred_element_type=jnp.float32,
+
+        def seats_all_name(block_in, a0):
+            which_axis = "col"
+            placed = axis_size(which_axis)
+            arr_now = axis_index(which_axis)
+            ledger = []
+            near, new, known = (placed, arr_now, block_in.shape[3])
+            for nth in range(near):
+                ledger.append((nth, (nth + 1) % near))
+            entries = []
+            for nth in range(near):
+                entries.append((nth, (nth - 1) % near))
+            big = near // 2
+            piece_out = block_last = block_in
+            y = a0(block_in, new * known)
+            for to_i in range(1, big + 1):
+                piece_out = ppermute(piece_out, which_axis, perm=ledger)
+                if to_i < near - big:
+                    block_last = ppermute(block_last, axis_name=which_axis, perm=entries)
+                    earlier = a0(block_last, (new + to_i) % near * known)
+                    y = y + earlier
+                y_new = a0(piece_out, (new - to_i) % near * known)
+                y = y + y_new
+            return y
+
+        image = seats_all_name(
+            ancestors,
+            lambda own_block, start: jnp.einsum(
+                "kajp,jpl->kal",
+                own_block,
+                lax.dynamic_slice_in_dim(stacked, start, own_block.shape[3], axis=1),
+                precision=highest,
+                preferred_element_type=jnp.float32,
+            ),
         )
         flat_image = image.reshape(brows * width, bcols * width)
         update = lax.psum_scatter(

time: 455 us -> 475 us (1.044); the launches traced: 454 us -> 468 us
  waiting for transfers between devices: 338 us -> 255 us
  starting transfers between devices: 0.21 us -> 79.6 us
  matrix products: 47.5 us -> 61.3 us
    ppermute x0 -> x30, waiting for transfers between devices: none -> 130 us  [the longest x16 119 us: seats_all_name(): piece_out = ppermute(piece_out, which_axis, perm=ledger)]
    all_gather x2 -> x0, waiting for transfers between devices: 121 us -> none  [shards(): lax.all_gather(ancestors, 'col', axis=3, tiled=True)]
    ppermute x0 -> x30, starting transfers between devices: none -> 79.5 us  [the longest x14 75.4 us: seats_all_name(): block_last = ppermute(block_last, axis_name=which_axis, perm=entries)]
    all_gather x1, waiting for transfers between devices: 113 us -> 46.9 us  [shards(): lax.all_gather(unit_factor, 'col', axis=3, tiled=True)]
    all_gather x1, waiting for transfers between devices: 29.4 us -> 0.02 us  [shards(): lax.all_gather(unit_factor, 'row', axis=1, tiled=True)]
    dot_general x2 -> x32, matrix products: 22.9 us -> 35 us  [shards(): jnp.einsum('kajp,jpl->kal', own_block, lax.dynamic_slice_in_dim(stacked,...]
    mul x0 -> x1, other arithmetic: none -> 5.68 us  [shards(): column_panel * jnp.repeat(struct, width)[:, None]]
  transfers between devices with their start and end apart: 6 -> 34, of which waited for: 6 -> 21; matrix products, arithmetic and copies ran while one was open for 11% -> 14% of each run, Pallas kernels for 0% -> 0%
where the time goes in v1:
time: 475 us; the launch traced here: 468 us
  waiting for transfers between devices  255 us (54%)
  starting transfers between devices  79.6 us (17%)
  matrix products  61.3 us (13%)
  local copies, waits for them, and re-layouts  37.7 us (8%)
  other arithmetic  20 us (4%)
  between operations  14.1 us (3%)
    ppermute x16, waiting for transfers between devices, seats_all_name(): piece_out = ppermute(piece_out, which_axis, perm=ledger)  119 us
    reduce_scatter x2, waiting for transfers between devices, shards(): lax.psum_scatter(jnp.einsum('hkp,hl->pkl', spread, flat_image - flat_ance...  76.9 us
    ppermute x14, starting transfers between devices, seats_all_name(): block_last = ppermute(block_last, axis_name=which_axis, perm=entries)  75.4 us
    all_gather x1, waiting for transfers between devices, shards(): lax.all_gather(unit_factor, 'col', axis=3, tiled=True)  46.9 us
    dot_general x32, matrix products, shards(): jnp.einsum('kajp,jpl->kal', own_block, lax.dynamic_slice_in_dim(stacked,...  35 us
    dot_general x2, matrix products, shards(): jnp.einsum('hkp,hl->pkl', spread, flat_image - flat_ancestors, precision=...  26.3 us
    mul x4, local copies, waits for them, and re-layouts, shards(): row_panel * jnp.repeat(pick(struct, row_ids), width)[:, None]  25.2 us
    ppermute x14, waiting for transfers between devices, seats_all_name(): block_last = ppermute(block_last, axis_name=which_axis, perm=entries)  11.1 us
  transfers between devices with their start and end apart: 34, of which 21 were waited for; matrix products, arithmetic and copies ran while one was open for 14% of the time, Pallas kernels for 0%

profile of v1, /device:TPU:0, one launch (start us, length us, event | category | flops | bytes accessed | tf_op | source)
XLA Modules:
  0.0 468.1 jit_solution(7832454793619783634)
XLA Ops:
  18.0 11.8 %collective-permute-done.1 = f32[4,128,2,128]{3,1,2,0:T(8,128)S(1)} collective-permute-done((f32[4,128,2,128]{3,1,2,0:T(8,128)S(1)}, f32[4,128,2,128]{3,1,2,0:T(8,128)S(1)}, u32[]{:S(2)}, u32[]{:S(2)}) %collective-permute-start.1) | collective-permute-done | bytes 524320 | tf_op jit(solution)/shard_map/ppermute | solution.py:73
  29.8 5.3 %collective-permute-start.2 = (f32[4,128,2,128]{3,1,2,0:T(8,128)S(1)}, f32[4,128,2,128]{3,1,2,0:T(8,128)S(1)}, u32[]{:S(2)}, u32[]{:S(2)}) collective-permute-start(f32[4,128,2,128]{3,1,2,0:T(8,128)S(1)} %collective-permute-done), channel_id=1, source_target_pairs={{0,15},{1,0},{2,1},{3,2},{4,3},{5,4},{6,5},{7,6},{8,7},{9,8},{10,9... | collective-permute-start | bytes 1572872 | tf_op jit(solution)/shard_map/ppermute | solution.py:75
  35.2 11.1 %collective-permute-done.3 = f32[4,128,2,128]{3,1,2,0:T(8,128)S(1)} collective-permute-done((f32[4,128,2,128]{3,1,2,0:T(8,128)S(1)}, f32[4,128,2,128]{3,1,2,0:T(8,128)S(1)}, u32[]{:S(2)}, u32[]{:S(2)}) %collective-permute-start.3) | collective-permute-done | bytes 524320 | tf_op jit(solution)/shard_map/ppermute | solution.py:73
  46.2 5.3 %collective-permute-start.4 = (f32[4,128,2,128]{3,1,2,0:T(8,128)S(1)}, f32[4,128,2,128]{3,1,2,0:T(8,128)S(1)}, u32[]{:S(2)}, u32[]{:S(2)}) collective-permute-start(f32[4,128,2,128]{3,1,2,0:T(8,128)S(1)} %collective-permute-done.2), channel_id=1, source_target_pairs={{0,15},{1,0},{2,1},{3,2},{4,3},{5,4},{6,5},{7,6},{8,7},{9,8},{10,9... | collective-permute-start | bytes 1572872 | tf_op jit(solution)/shard_map/ppermute | solution.py:75
  51.6 10.2 %collective-permute-done.5 = f32[4,128,2,128]{3,1,2,0:T(8,128)S(1)} collective-permute-done((f32[4,128,2,128]{3,1,2,0:T(8,128)S(1)}, f32[4,128,2,128]{3,1,2,0:T(8,128)S(1)}, u32[]{:S(2)}, u32[]{:S(2)}) %collective-permute-start.5) | collective-permute-done | bytes 524320 | tf_op jit(solution)/shard_map/ppermute | solution.py:73
  61.8 5.7 %collective-permute-done.4 = f32[4,128,2,128]{3,1,2,0:T(8,128)S(1)} collective-permute-done((f32[4,128,2,128]{3,1,2,0:T(8,128)S(1)}, f32[4,128,2,128]{3,1,2,0:T(8,128)S(1)}, u32[]{:S(2)}, u32[]{:S(2)}) %collective-permute-start.4) | collective-permute-done | bytes 524320 | tf_op jit(solution)/shard_map/ppermute | solution.py:75
  67.5 5.8 %collective-permute-start.6 = (f32[4,128,2,128]{3,1,2,0:T(8,128)S(1)}, f32[4,128,2,128]{3,1,2,0:T(8,128)}, u32[]{:S(2)}, u32[]{:S(2)}) collective-permute-start(f32[4,128,2,128]{3,1,2,0:T(8,128)S(1)} %collective-permute-done.4), channel_id=1, source_target_pairs={{0,15},{1,0},{2,1},{3,2},{4,3},{5,4},{6,5},{7,6},{8,7},{9,8},{10,9... | collective-permute-start | bytes 1572872 | tf_op jit(solution)/shard_map/ppermute | solution.py:75
  73.3 10.9 %collective-permute-done.7 = f32[4,128,2,128]{3,1,2,0:T(8,128)S(1)} collective-permute-done((f32[4,128,2,128]{3,1,2,0:T(8,128)S(1)}, f32[4,128,2,128]{3,1,2,0:T(8,128)S(1)}, u32[]{:S(2)}, u32[]{:S(2)}) %collective-permute-start.7) | collective-permute-done | bytes 524320 | tf_op jit(solution)/shard_map/ppermute | solution.py:73
  86.0 5.9 %collective-permute-start.8 = (f32[4,128,2,128]{3,1,2,0:T(8,128)}, f32[4,128,2,128]{3,1,2,0:T(8,128)}, u32[]{:S(2)}, u32[]{:S(2)}) collective-permute-start(f32[4,128,2,128]{3,1,2,0:T(8,128)} %collective-permute-done.6), channel_id=1, source_target_pairs={{0,15},{1,0},{2,1},{3,2},{4,3},{5,4},{6,5},{7,6},{8,7},{9,8},{10,9... | collective-permute-start | bytes 1572872 | tf_op jit(solution)/shard_map/ppermute | solution.py:75
  91.9 10.2 %collective-permute-done.9 = f32[4,128,2,128]{3,1,2,0:T(8,128)} collective-permute-done((f32[4,128,2,128]{3,1,2,0:T(8,128)S(1)}, f32[4,128,2,128]{3,1,2,0:T(8,128)}, u32[]{:S(2)}, u32[]{:S(2)}) %collective-permute-start.9) | collective-permute-done | bytes 524320 | tf_op jit(solution)/shard_map/ppermute | solution.py:73
  102.5 5.3 %collective-permute-start.10 = (f32[4,128,2,128]{3,1,2,0:T(8,128)}, f32[4,128,2,128]{3,1,2,0:T(8,128)}, u32[]{:S(2)}, u32[]{:S(2)}) collective-permute-start(f32[4,128,2,128]{3,1,2,0:T(8,128)} %collective-permute-done.8), channel_id=1, source_target_pairs={{0,15},{1,0},{2,1},{3,2},{4,3},{5,4},{6,5},{7,6},{8,7},{9,8},{10,9... | collective-permute-start | bytes 1572872 | tf_op jit(solution)/shard_map/ppermute | solution.py:75
  107.8 10.6 %collective-permute-done.11 = f32[4,128,2,128]{3,1,2,0:T(8,128)} collective-permute-done((f32[4,128,2,128]{3,1,2,0:T(8,128)}, f32[4,128,2,128]{3,1,2,0:T(8,128)}, u32[]{:S(2)}, u32[]{:S(2)}) %collective-permute-start.11) | collective-permute-done | bytes 524320 | tf_op jit(solution)/shard_map/ppermute | solution.py:73
  124.3 9.4 %collective-permute-done.13 = f32[4,128,2,128]{3,1,2,0:T(8,128)} collective-permute-done((f32[4,128,2,128]{3,1,2,0:T(8,128)}, f32[4,128,2,128]{3,1,2,0:T(8,128)}, u32[]{:S(2)}, u32[]{:S(2)}) %collective-permute-start.13) | collective-permute-done | bytes 524320 | tf_op jit(solution)/shard_map/ppermute | solution.py:73
  133.9 6.4 %reshape.289 = f32[2,2048,256]{2,1,0:T(8,128)} reshape(f32[4,1024,2,128]{3,2,1,0:T(2,128)} %all-gather.3.cloned.1.call-done) | data formatting | bytes 8388608 | tf_op jit(solution)/shard_map/reshape | solution.py:35
  140.4 5.7 %multiply_multiply_fusion.2 = (f32[2,2048,256]{2,1,0:T(8,128)}, f32[2,2048,256]{2,1,0:T(8,128)S(1)}) fusion(f32[2,2048,256]{2,1,0:T(8,128)} %reshape.289, f32[256]{0:T(256)S(1)} %get-tuple-element.32, f32[2,2048]{1,0:T(2,128)S(1)} %get-tuple-element.34, f32[256]{0:T(256)S(1)} %get-tuple-element.33, f32[2,2048]{1,0:T(2,128)S(1)} %get-tuple-element.35), kind=kLoop, calls=%fused_computation.6 | loop fusion | flops 4194304 | bytes 12617728 | tf_op jit(solution)/shard_map/mul | solution.py:45
  164.0 46.9 %all-gather.5.cloned.1.call-done = f32[4,128,2,2048]{3,2,1,0:T(2,128)} async-done(((f32[4,128,2,128]{3,2,1,0:T(2,128)}), f32[4,128,2,2048]{3,2,1,0:T(2,128)}) %all-gather.5.cloned.1.call-update) | async-done | bytes 8388624 | tf_op jit(solution)/shard_map/all_gather | solution.py:38
  210.9 10.5 %multiply_multiply_fusion = (f32[4,128,2,2048]{3,2,1,0:T(2,128)}, f32[4,128,2,2048]{3,2,1,0:T(2,128)}) fusion(f32[4,128,2,2048]{3,2,1,0:T(2,128)} %all-gather.5.cloned.1.call-done, f32[4]{0:T(128)S(1)} %get-tuple-element.6, f32[2,2048]{1,0:T(2,128)S(1)} %mul.368, f32[2,2048]{1,0:T(2,128)S(1)} %mul.347, f32[4]{0:T(128)S(1)} %get-tuple-element.8), kind=kLoop, calls=%fused_computation.4 | loop fusion | flops 8388608 | bytes 25198624 | tf_op jit(solution)/shard_map/mul | solution.py:50
  221.4 12.7 %mul.350 = f32[512,4,1024]{2,1,0:T(4,128)} reshape(f32[4,128,2,2048]{3,2,1,0:T(2,128)} %get-tuple-element.16) | data formatting | bytes 16777216 | tf_op jit(solution)/shard_map/mul | solution.py:50
  234.1 14.2 %fusion.4 = f32[1024,4,256]{0,2,1:T(8,128)} fusion(f32[512,256,1]{1,0,2:T(8,128)S(1)} %bitcast.346, f32[512,4,1024]{2,1,0:T(4,128)} %mul.350), kind=kOutput, calls=%fused_computation.8 | convolution fusion | flops 6442450944 | bytes 13107200 | tf_op jit(solution)/shard_map/hkp,hl->pkl/dot_general | solution.py:94
  248.4 36.3 %reduce-scatter.3.cloned.1.call-done = f32[128,4,256]{0,2,1:T(8,128)} async-done(((f32[1024,4,256]{0,2,1:T(8,128)}), f32[128,4,256]{0,2,1:T(8,128)}) %reduce-scatter.3.cloned.1.call-update) | async-done | bytes 524304 | tf_op jit(solution)/shard_map/reduce_scatter | solution.py:93
  291.6 8.8 %collective-permute-done.16 = f32[4,128,2,128]{3,1,2,0:T(8,128)S(1)} collective-permute-done((f32[4,128,2,128]{3,1,2,0:T(8,128)S(1)}, f32[4,128,2,128]{3,1,2,0:T(8,128)S(1)}, u32[]{:S(2)}, u32[]{:S(2)}) %collective-permute-start.16) | collective-permute-done | bytes 524320 | tf_op jit(solution)/shard_map/ppermute | solution.py:73
  306.5 7.2 %collective-permute-done.18 = f32[4,128,2,128]{3,1,2,0:T(8,128)} collective-permute-done((f32[4,128,2,128]{3,1,2,0:T(8,128)S(1)}, f32[4,128,2,128]{3,1,2,0:T(8,128)}, u32[]{:S(2)}, u32[]{:S(2)}) %collective-permute-start.18) | collective-permute-done | bytes 524320 | tf_op jit(solution)/shard_map/ppermute | solution.py:73
  313.8 5.9 %collective-permute-start.19 = (f32[4,128,2,128]{3,1,2,0:T(8,128)}, f32[4,128,2,128]{3,1,2,0:T(8,128)}, u32[]{:S(2)}, u32[]{:S(2)}) collective-permute-start(f32[4,128,2,128]{3,1,2,0:T(8,128)} %collective-permute-done.17), channel_id=1, source_target_pairs={{0,15},{1,0},{2,1},{3,2},{4,3},{5,4},{6,5},{7,6},{8,7},{9,8},{10,9... | collective-permute-start | bytes 1572872 | tf_op jit(solution)/shard_map/ppermute | solution.py:75
  319.6 12.5 %mul.371 = f32[512,4,1024]{2,1,0:T(4,128)} reshape(f32[4,128,2,2048]{3,2,1,0:T(2,128)} %get-tuple-element.15) | data formatting | bytes 16777216 | tf_op jit(solution)/shard_map/mul | solution.py:50
  349.6 5.6 %collective-permute-start.23 = (f32[4,128,2,128]{3,1,2,0:T(8,128)S(1)}, f32[4,128,2,128]{3,1,2,0:T(8,128)S(1)}, u32[]{:S(2)}, u32[]{:S(2)}) collective-permute-start(f32[4,128,2,128]{3,1,2,0:T(8,128)S(1)} %collective-permute-done.21), channel_id=1, source_target_pairs={{0,15},{1,0},{2,1},{3,2},{4,3},{5,4},{6,5},{7,6},{8,7},{9,8},{10,9... | collective-permute-start | bytes 1572872 | tf_op jit(solution)/shard_map/ppermute | solution.py:75
  363.8 5.8 %collective-permute-start.25 = (f32[4,128,2,128]{3,1,2,0:T(8,128)S(1)}, f32[4,128,2,128]{3,1,2,0:T(8,128)S(1)}, u32[]{:S(2)}, u32[]{:S(2)}) collective-permute-start(f32[4,128,2,128]{3,1,2,0:T(8,128)S(1)} %collective-permute-done.23), channel_id=1, source_target_pairs={{0,15},{1,0},{2,1},{3,2},{4,3},{5,4},{6,5},{7,6},{8,7},{9,8},{10,9... | collective-permute-start | bytes 1572872 | tf_op jit(solution)/shard_map/ppermute | solution.py:75
  370.2 5.5 %collective-permute-done.26 = f32[4,128,2,128]{3,1,2,0:T(8,128)S(1)} collective-permute-done((f32[4,128,2,128]{3,1,2,0:T(8,128)S(1)}, f32[4,128,2,128]{3,1,2,0:T(8,128)S(1)}, u32[]{:S(2)}, u32[]{:S(2)}) %collective-permute-start.26) | collective-permute-done | bytes 524320 | tf_op jit(solution)/shard_map/ppermute | solution.py:73
  379.4 5.8 %collective-permute-start.27 = (f32[4,128,2,128]{3,1,2,0:T(8,128)S(1)}, f32[4,128,2,128]{3,1,2,0:T(8,128)S(1)}, u32[]{:S(2)}, u32[]{:S(2)}) collective-permute-start(f32[4,128,2,128]{3,1,2,0:T(8,128)S(1)} %collective-permute-done.25), channel_id=1, source_target_pairs={{0,15},{1,0},{2,1},{3,2},{4,3},{5,4},{6,5},{7,6},{8,7},{9,8},{10,9... | collective-permute-start | bytes 1572872 | tf_op jit(solution)/shard_map/ppermute | solution.py:75
  385.8 6.3 %collective-permute-done.28 = f32[4,128,2,128]{3,1,2,0:T(8,128)S(1)} collective-permute-done((f32[4,128,2,128]{3,1,2,0:T(8,128)S(1)}, f32[4,128,2,128]{3,1,2,0:T(8,128)S(1)}, u32[]{:S(2)}, u32[]{:S(2)}) %collective-permute-start.28) | collective-permute-done | bytes 524320 | tf_op jit(solution)/shard_map/ppermute | solution.py:73
  394.1 10.6 %collective-permute-done.29 = f32[4,128,2,128]{3,1,2,0:T(8,128)S(1)} collective-permute-done((f32[4,128,2,128]{3,1,2,0:T(8,128)S(1)}, f32[4,128,2,128]{3,1,2,0:T(8,128)S(1)}, u32[]{:S(2)}, u32[]{:S(2)}) %collective-permute-start.29) | collective-permute-done | bytes 524320 | tf_op jit(solution)/shard_map/ppermute | solution.py:73
  405.4 12.2 %fusion.7 = f32[1024,4,256]{0,2,1:T(8,128)} fusion(f32[512,256,1]{1,0,2:T(8,128)S(1)} %bitcast.347, f32[512,4,1024]{2,1,0:T(4,128)S(1)} %bitcast.345), kind=kOutput, calls=%fused_computation.9 | convolution fusion | flops 6442450944 | bytes 13107200 | tf_op jit(solution)/shard_map/hkp,hl->pkl/dot_general | solution.py:94
  418.0 40.6 %reduce-scatter.5.cloned.1.call-done = f32[128,4,256]{0,2,1:T(8,128)} async-done(((f32[1024,4,256]{0,2,1:T(8,128)}), f32[128,4,256]{0,2,1:T(8,128)}) %reduce-scatter.5.cloned.1.call-update) | async-done | bytes 524304 | tf_op jit(solution)/shard_map/reduce_scatter | solution.py:93
  (131 shorter events, 86.9 us)
Async XLA Ops:
  6.5 127.4 %all-gather.3.cloned.1.call-start = ((), (), s32[]{:S(2)}) async-start(), calls=%async_computation.2 | async-start | bytes 4718592 | tf_op jit(solution)/shard_map/all_gather | solution.py:35
  7.3 203.6 %all-gather.5.cloned.1.call-start = ((), (), s32[]{:S(2)}) async-start(), calls=%async_computation.3 | async-start | bytes 8912896 | tf_op jit(solution)/shard_map/all_gather | solution.py:38
  8.0 276.7 %reduce-scatter.3.cloned.1.call-start = ((), (), s32[]{:S(2)}) async-start(), calls=%async_computation.4 | async-start | bytes 4718592 | tf_op jit(solution)/shard_map/reduce_scatter | solution.py:93
  11.2 18.6 %collective-permute-start.1 = (f32[4,128,2,128]{3,1,2,0:T(8,128)S(1)}, f32[4,128,2,128]{3,1,2,0:T(8,128)S(1)}, u32[]{:S(2)}, u32[]{:S(2)}) collective-permute-start(f32[4,128,2,128]{3,1,2,0:T(8,128)S(1)} %multiply_multiply_fusion.4), channel_id=1, source_target_pairs={{0,1},{1,2},{2,3},{3,4},{4,5},{5,6},{6,7},{7,8},{8,9},{9,10},{10,1... | collective-permute-start | bytes 1572872 | tf_op jit(solution)/shard_map/ppermute | solution.py:73
  13.0 16.8 %collective-permute-start = (f32[4,128,2,128]{3,1,2,0:T(8,128)S(1)}, f32[4,128,2,128]{3,1,2,0:T(8,128)S(1)}, u32[]{:S(2)}, u32[]{:S(2)}) collective-permute-start(f32[4,128,2,128]{3,1,2,0:T(8,128)S(1)} %multiply_multiply_fusion.4), channel_id=1, source_target_pairs={{0,15},{1,0},{2,1},{3,2},{4,3},{5,4},{6,5},{7,6},{8,7},{9,8},{10,9... | collective-permute-start | bytes 1572872 | tf_op jit(solution)/shard_map/ppermute | solution.py:75
  29.8 16.4 %collective-permute-start.3 = (f32[4,128,2,128]{3,1,2,0:T(8,128)S(1)}, f32[4,128,2,128]{3,1,2,0:T(8,128)S(1)}, u32[]{:S(2)}, u32[]{:S(2)}) collective-permute-start(f32[4,128,2,128]{3,1,2,0:T(8,128)S(1)} %collective-permute-done.1), channel_id=1, source_target_pairs={{0,1},{1,2},{2,3},{3,4},{4,5},{5,6},{6,7},{7,8},{8,9},{9,10},{10,1... | collective-permute-start | bytes 1572872 | tf_op jit(solution)/shard_map/ppermute | solution.py:73
  29.8 16.4 %collective-permute-start.2 = (f32[4,128,2,128]{3,1,2,0:T(8,128)S(1)}, f32[4,128,2,128]{3,1,2,0:T(8,128)S(1)}, u32[]{:S(2)}, u32[]{:S(2)}) collective-permute-start(f32[4,128,2,128]{3,1,2,0:T(8,128)S(1)} %collective-permute-done), channel_id=1, source_target_pairs={{0,15},{1,0},{2,1},{3,2},{4,3},{5,4},{6,5},{7,6},{8,7},{9,8},{10,9... | collective-permute-start | bytes 1572872 | tf_op jit(solution)/shard_map/ppermute | solution.py:75
  46.2 15.6 %collective-permute-start.5 = (f32[4,128,2,128]{3,1,2,0:T(8,128)S(1)}, f32[4,128,2,128]{3,1,2,0:T(8,128)S(1)}, u32[]{:S(2)}, u32[]{:S(2)}) collective-permute-start(f32[4,128,2,128]{3,1,2,0:T(8,128)S(1)} %collective-permute-done.3), channel_id=1, source_target_pairs={{0,1},{1,2},{2,3},{3,4},{4,5},{5,6},{6,7},{7,8},{8,9},{9,10},{10,1... | collective-permute-start | bytes 1572872 | tf_op jit(solution)/shard_map/ppermute | solution.py:73
  46.2 21.3 %collective-permute-start.4 = (f32[4,128,2,128]{3,1,2,0:T(8,128)S(1)}, f32[4,128,2,128]{3,1,2,0:T(8,128)S(1)}, u32[]{:S(2)}, u32[]{:S(2)}) collective-permute-start(f32[4,128,2,128]{3,1,2,0:T(8,128)S(1)} %collective-permute-done.2), channel_id=1, source_target_pairs={{0,15},{1,0},{2,1},{3,2},{4,3},{5,4},{6,5},{7,6},{8,7},{9,8},{10,9... | collective-permute-start | bytes 1572872 | tf_op jit(solution)/shard_map/ppermute | solution.py:75
  61.8 22.4 %collective-permute-start.7 = (f32[4,128,2,128]{3,1,2,0:T(8,128)S(1)}, f32[4,128,2,128]{3,1,2,0:T(8,128)S(1)}, u32[]{:S(2)}, u32[]{:S(2)}) collective-permute-start(f32[4,128,2,128]{3,1,2,0:T(8,128)S(1)} %collective-permute-done.5), channel_id=1, source_target_pairs={{0,1},{1,2},{2,3},{3,4},{4,5},{5,6},{6,7},{7,8},{8,9},{9,10},{10,1... | collective-permute-start | bytes 1572872 | tf_op jit(solution)/shard_map/ppermute | solution.py:73
  67.5 18.5 %collective-permute-start.6 = (f32[4,128,2,128]{3,1,2,0:T(8,128)S(1)}, f32[4,128,2,128]{3,1,2,0:T(8,128)}, u32[]{:S(2)}, u32[]{:S(2)}) collective-permute-start(f32[4,128,2,128]{3,1,2,0:T(8,128)S(1)} %collective-permute-done.4), channel_id=1, source_target_pairs={{0,15},{1,0},{2,1},{3,2},{4,3},{5,4},{6,5},{7,6},{8,7},{9,8},{10,9... | collective-permute-start | bytes 1572872 | tf_op jit(solution)/shard_map/ppermute | solution.py:75
  84.2 18.0 %collective-permute-start.9 = (f32[4,128,2,128]{3,1,2,0:T(8,128)S(1)}, f32[4,128,2,128]{3,1,2,0:T(8,128)}, u32[]{:S(2)}, u32[]{:S(2)}) collective-permute-start(f32[4,128,2,128]{3,1,2,0:T(8,128)S(1)} %collective-permute-done.7), channel_id=1, source_target_pairs={{0,1},{1,2},{2,3},{3,4},{4,5},{5,6},{6,7},{7,8},{8,9},{9,10},{10,1... | collective-permute-start | bytes 1572872 | tf_op jit(solution)/shard_map/ppermute | solution.py:73
  86.0 16.4 %collective-permute-start.8 = (f32[4,128,2,128]{3,1,2,0:T(8,128)}, f32[4,128,2,128]{3,1,2,0:T(8,128)}, u32[]{:S(2)}, u32[]{:S(2)}) collective-permute-start(f32[4,128,2,128]{3,1,2,0:T(8,128)} %collective-permute-done.6), channel_id=1, source_target_pairs={{0,15},{1,0},{2,1},{3,2},{4,3},{5,4},{6,5},{7,6},{8,7},{9,8},{10,9... | collective-permute-start | bytes 1572872 | tf_op jit(solution)/shard_map/ppermute | solution.py:75
  102.2 16.2 %collective-permute-start.11 = (f32[4,128,2,128]{3,1,2,0:T(8,128)}, f32[4,128,2,128]{3,1,2,0:T(8,128)}, u32[]{:S(2)}, u32[]{:S(2)}) collective-permute-start(f32[4,128,2,128]{3,1,2,0:T(8,128)} %collective-permute-done.9), channel_id=1, source_target_pairs={{0,1},{1,2},{2,3},{3,4},{4,5},{5,6},{6,7},{7,8},{8,9},{9,10},{10,1... | collective-permute-start | bytes 1572872 | tf_op jit(solution)/shard_map/ppermute | solution.py:73
  102.5 16.6 %collective-permute-start.10 = (f32[4,128,2,128]{3,1,2,0:T(8,128)}, f32[4,128,2,128]{3,1,2,0:T(8,128)}, u32[]{:S(2)}, u32[]{:S(2)}) collective-permute-start(f32[4,128,2,128]{3,1,2,0:T(8,128)} %collective-permute-done.8), channel_id=1, source_target_pairs={{0,15},{1,0},{2,1},{3,2},{4,3},{5,4},{6,5},{7,6},{8,7},{9,8},{10,9... | collective-permute-start | bytes 1572872 | tf_op jit(solution)/shard_map/ppermute | solution.py:75
  118.4 15.4 %collective-permute-start.13 = (f32[4,128,2,128]{3,1,2,0:T(8,128)}, f32[4,128,2,128]{3,1,2,0:T(8,128)}, u32[]{:S(2)}, u32[]{:S(2)}) collective-permute-start(f32[4,128,2,128]{3,1,2,0:T(8,128)} %collective-permute-done.11), channel_id=1, source_target_pairs={{0,1},{1,2},{2,3},{3,4},{4,5},{5,6},{6,7},{7,8},{8,9},{9,10},{10,1... | collective-permute-start | bytes 1572872 | tf_op jit(solution)/shard_map/ppermute | solution.py:73
  119.1 41.6 %collective-permute-start.12 = (f32[4,128,2,128]{3,1,2,0:T(8,128)}, f32[4,128,2,128]{3,1,2,0:T(8,128)}, u32[]{:S(2)}, u32[]{:S(2)}) collective-permute-start(f32[4,128,2,128]{3,1,2,0:T(8,128)} %collective-permute-done.10), channel_id=1, source_target_pairs={{0,15},{1,0},{2,1},{3,2},{4,3},{5,4},{6,5},{7,6},{8,7},{9,8},{10,9... | collective-permute-start | bytes 1572872 | tf_op jit(solution)/shard_map/ppermute | solution.py:75
  133.7 28.6 %collective-permute-start.14 = (f32[4,128,2,128]{3,1,2,0:T(8,128)}, f32[4,128,2,128]{3,1,2,0:T(8,128)}, u32[]{:S(2)}, u32[]{:S(2)}) collective-permute-start(f32[4,128,2,128]{3,1,2,0:T(8,128)} %collective-permute-done.13), channel_id=1, source_target_pairs={{0,1},{1,2},{2,3},{3,4},{4,5},{5,6},{6,7},{7,8},{8,9},{9,10},{10,1... | collective-permute-start | bytes 1572872 | tf_op jit(solution)/shard_map/ppermute | solution.py:73
  248.3 210.4 %reduce-scatter.5.cloned.1.call-start = ((), (), s32[]{:S(2)}) async-start(), calls=%async_computation.5 | async-start | bytes 4718592 | tf_op jit(solution)/shard_map/reduce_scatter | solution.py:93
  286.2 14.2 %collective-permute-start.16 = (f32[4,128,2,128]{3,1,2,0:T(8,128)S(1)}, f32[4,128,2,128]{3,1,2,0:T(8,128)S(1)}, u32[]{:S(2)}, u32[]{:S(2)}) collective-permute-start(f32[4,128,2,128]{3,1,2,0:T(8,128)S(1)} %broadcast_multiply_fusion), channel_id=1, source_target_pairs={{0,1},{1,2},{2,3},{3,4},{4,5},{5,6},{6,7},{7,8},{8,9},{9,10},{10,1... | collective-permute-start | bytes 1572872 | tf_op jit(solution)/shard_map/ppermute | solution.py:73
  287.7 12.7 %collective-permute-start.15 = (f32[4,128,2,128]{3,1,2,0:T(8,128)S(1)}, f32[4,128,2,128]{3,1,2,0:T(8,128)S(1)}, u32[]{:S(2)}, u32[]{:S(2)}) collective-permute-start(f32[4,128,2,128]{3,1,2,0:T(8,128)S(1)} %broadcast_multiply_fusion), channel_id=1, source_target_pairs={{0,15},{1,0},{2,1},{3,2},{4,3},{5,4},{6,5},{7,6},{8,7},{9,8},{10,9... | collective-permute-start | bytes 1572872 | tf_op jit(solution)/shard_map/ppermute | solution.py:75
  300.4 13.4 %collective-permute-start.18 = (f32[4,128,2,128]{3,1,2,0:T(8,128)S(1)}, f32[4,128,2,128]{3,1,2,0:T(8,128)}, u32[]{:S(2)}, u32[]{:S(2)}) collective-permute-start(f32[4,128,2,128]{3,1,2,0:T(8,128)S(1)} %collective-permute-done.16), channel_id=1, source_target_pairs={{0,1},{1,2},{2,3},{3,4},{4,5},{5,6},{6,7},{7,8},{8,9},{9,10},{10,1... | collective-permute-start | bytes 1572872 | tf_op jit(solution)/shard_map/ppermute | solution.py:73
  313.8 18.8 %collective-permute-start.20 = (f32[4,128,2,128]{3,1,2,0:T(8,128)}, f32[4,128,2,128]{3,1,2,0:T(8,128)}, u32[]{:S(2)}, u32[]{:S(2)}) collective-permute-start(f32[4,128,2,128]{3,1,2,0:T(8,128)} %collective-permute-done.18), channel_id=1, source_target_pairs={{0,1},{1,2},{2,3},{3,4},{4,5},{5,6},{6,7},{7,8},{8,9},{9,10},{10,1... | collective-permute-start | bytes 1572872 | tf_op jit(solution)/shard_map/ppermute | solution.py:73
  313.8 22.8 %collective-permute-start.19 = (f32[4,128,2,128]{3,1,2,0:T(8,128)}, f32[4,128,2,128]{3,1,2,0:T(8,128)}, u32[]{:S(2)}, u32[]{:S(2)}) collective-permute-start(f32[4,128,2,128]{3,1,2,0:T(8,128)} %collective-permute-done.17), channel_id=1, source_target_pairs={{0,15},{1,0},{2,1},{3,2},{4,3},{5,4},{6,5},{7,6},{8,7},{9,8},{10,9... | collective-permute-start | bytes 1572872 | tf_op jit(solution)/shard_map/ppermute | solution.py:75
  332.6 13.7 %collective-permute-start.22 = (f32[4,128,2,128]{3,1,2,0:T(8,128)}, f32[4,128,2,128]{3,1,2,0:T(8,128)S(1)}, u32[]{:S(2)}, u32[]{:S(2)}) collective-permute-start(f32[4,128,2,128]{3,1,2,0:T(8,128)} %collective-permute-done.20), channel_id=1, source_target_pairs={{0,1},{1,2},{2,3},{3,4},{4,5},{5,6},{6,7},{7,8},{8,9},{9,10},{10,1... | collective-permute-start | bytes 1572872 | tf_op jit(solution)/shard_map/ppermute | solution.py:73
  336.6 13.0 %collective-permute-start.21 = (f32[4,128,2,128]{3,1,2,0:T(8,128)}, f32[4,128,2,128]{3,1,2,0:T(8,128)S(1)}, u32[]{:S(2)}, u32[]{:S(2)}) collective-permute-start(f32[4,128,2,128]{3,1,2,0:T(8,128)} %collective-permute-done.19), channel_id=1, source_target_pairs={{0,15},{1,0},{2,1},{3,2},{4,3},{5,4},{6,5},{7,6},{8,7},{9,8},{10,9... | collective-permute-start | bytes 1572872 | tf_op jit(solution)/shard_map/ppermute | solution.py:75
  346.3 14.2 %collective-permute-start.24 = (f32[4,128,2,128]{3,1,2,0:T(8,128)S(1)}, f32[4,128,2,128]{3,1,2,0:T(8,128)S(1)}, u32[]{:S(2)}, u32[]{:S(2)}) collective-permute-start(f32[4,128,2,128]{3,1,2,0:T(8,128)S(1)} %collective-permute-done.22), channel_id=1, source_target_pairs={{0,1},{1,2},{2,3},{3,4},{4,5},{5,6},{6,7},{7,8},{8,9},{9,10},{10,1... | collective-permute-start | bytes 1572872 | tf_op jit(solution)/shard_map/ppermute | solution.py:73
  349.6 14.2 %collective-permute-start.23 = (f32[4,128,2,128]{3,1,2,0:T(8,128)S(1)}, f32[4,128,2,128]{3,1,2,0:T(8,128)S(1)}, u32[]{:S(2)}, u32[]{:S(2)}) collective-permute-start(f32[4,128,2,128]{3,1,2,0:T(8,128)S(1)} %collective-permute-done.21), channel_id=1, source_target_pairs={{0,15},{1,0},{2,1},{3,2},{4,3},{5,4},{6,5},{7,6},{8,7},{9,8},{10,9... | collective-permute-start | bytes 1572872 | tf_op jit(solution)/shard_map/ppermute | solution.py:75
  360.4 15.3 %collective-permute-start.26 = (f32[4,128,2,128]{3,1,2,0:T(8,128)S(1)}, f32[4,128,2,128]{3,1,2,0:T(8,128)S(1)}, u32[]{:S(2)}, u32[]{:S(2)}) collective-permute-start(f32[4,128,2,128]{3,1,2,0:T(8,128)S(1)} %collective-permute-done.24), channel_id=1, source_target_pairs={{0,1},{1,2},{2,3},{3,4},{4,5},{5,6},{6,7},{7,8},{8,9},{9,10},{10,1... | collective-permute-start | bytes 1572872 | tf_op jit(solution)/shard_map/ppermute | solution.py:73
  363.8 15.6 %collective-permute-start.25 = (f32[4,128,2,128]{3,1,2,0:T(8,128)S(1)}, f32[4,128,2,128]{3,1,2,0:T(8,128)S(1)}, u32[]{:S(2)}, u32[]{:S(2)}) collective-permute-start(f32[4,128,2,128]{3,1,2,0:T(8,128)S(1)} %collective-permute-done.23), channel_id=1, source_target_pairs={{0,15},{1,0},{2,1},{3,2},{4,3},{5,4},{6,5},{7,6},{8,7},{9,8},{10,9... | collective-permute-start | bytes 1572872 | tf_op jit(solution)/shard_map/ppermute | solution.py:75
  375.8 16.3 %collective-permute-start.28 = (f32[4,128,2,128]{3,1,2,0:T(8,128)S(1)}, f32[4,128,2,128]{3,1,2,0:T(8,128)S(1)}, u32[]{:S(2)}, u32[]{:S(2)}) collective-permute-start(f32[4,128,2,128]{3,1,2,0:T(8,128)S(1)} %collective-permute-done.26), channel_id=1, source_target_pairs={{0,1},{1,2},{2,3},{3,4},{4,5},{5,6},{6,7},{7,8},{8,9},{9,10},{10,1... | collective-permute-start | bytes 1572872 | tf_op jit(solution)/shard_map/ppermute | solution.py:73
  379.4 14.1 %collective-permute-start.27 = (f32[4,128,2,128]{3,1,2,0:T(8,128)S(1)}, f32[4,128,2,128]{3,1,2,0:T(8,128)S(1)}, u32[]{:S(2)}, u32[]{:S(2)}) collective-permute-start(f32[4,128,2,128]{3,1,2,0:T(8,128)S(1)} %collective-permute-done.25), channel_id=1, source_target_pairs={{0,15},{1,0},{2,1},{3,2},{4,3},{5,4},{6,5},{7,6},{8,7},{9,8},{10,9... | collective-permute-start | bytes 1572872 | tf_op jit(solution)/shard_map/ppermute | solution.py:75
  (12 other events, 151.3 us)
Sparse Core Ops, SparseCore 0:
  9.0 34.4 all-gather.2
  45.7 165.1 all-gather.4
  248.4 36.2 reduce-scatter.2
  417.7 40.9 reduce-scatter.4
